TPU v7x, 32 devices: a whole 2x2x4 slice. The times are simulated.
32 devices in a mesh: grad: 4 (over y, x), col: 8 (over z, core).
Axes of the slice: x: 2, y: 2, z: 4, core: 2. Of those that a mesh axis runs over, the one named last changes fastest.
Arguments:
- gradient: bfloat16 [16384, 53248], P(('grad', 'col'))
- test_matrix: bfloat16 [16384, 256], P(('grad', 'col')), may hold values from -6 to 6
Outputs:
- low_rank: float32 [16384, 256], P(('grad', 'col'))
- projector: float32 [53248, 256], P('col')
All inputs are finite; a program needn't handle non-finite values.
Results may differ from a plain program's by a relative error of at most 0.008.
Values may be sent and summed in bfloat16 or wider, within the bound.
No kernel may reach another device: no remote copies, remote signals or barrier semaphores. Data moves between devices by JAX's collectives and lax.ppermute only.
A program may use at most 256 MiB of HBM per device.

v0:
```python
import math
import jax
import jax.numpy as jnp
from jax import lax
from jax.sharding import PartitionSpec as P

FF = 53248
POWER = 2


def orthonormal(matrix, reduce_gram):
    partial_gram = lax.dot_general(
        matrix,
        matrix,
        (((0,), (0,)), ((), ())),
        precision=lax.Precision.HIGHEST,
        preferred_element_type=jnp.float32,
    )
    gram = reduce_gram(partial_gram)
    lower_factor = jnp.linalg.cholesky(gram)
    return lax.linalg.triangular_solve(
        lower_factor, matrix, left_side=False, lower=True, transpose_a=True
    )


def gram_over_columns(partial_gram):
    return lax.psum(partial_gram, "col")


def shards(gradient, test_matrix):
    blocks = lax.all_to_all(gradient, "col", split_axis=1, concat_axis=0, tiled=True)

    def add_sketch(row_piece):
        return lax.dot_general(
            blocks, row_piece, (((0,), (0,)), ((), ())), preferred_element_type=jnp.float32
        )

    sketch = add_sketch(lax.all_gather(test_matrix, "col", axis=0, tiled=True))
    for iteration in range(POWER + 1):
        summed = lax.psum(sketch, "grad")
        basis_block = orthonormal(summed, gram_over_columns)
        basis_bf = basis_block.astype(jnp.bfloat16)
        reduced = lax.psum_scatter(
            jnp.dot(blocks, basis_bf, preferred_element_type=jnp.float32),
            "col",
            scatter_dimension=0,
            tiled=True,
        )
        if iteration < POWER:
            reduced_bf = reduced.astype(jnp.bfloat16)
            sketch = add_sketch(lax.all_gather(reduced_bf, "col", axis=0, tiled=True))
    return (reduced, basis_block * math.sqrt(FF))


def solution(mesh):
    return jax.shard_map(
        shards,
        mesh=mesh,
        in_specs=(P(("grad", "col"), None), P(("grad", "col"), None)),
        out_specs=(P(("grad", "col"), None), P("col", None)),
        check_vma=False,
    )
```

profile of v0, /device:TPU:0, one launch (start us, length us, event | category | flops | bytes accessed | tf_op | source)
XLA Modules:
  0.0 2602.8 jit_solution(11232503956803364355)
XLA Ops:
  7.2 70.6 %copy.20 = bf16[512,53248]{0,1:T(8,128)(2,1)} copy(bf16[512,53248]{1,0:T(8,128)(2,1)} %param.5) | data formatting | bytes 109051904 | tf_op args[0]
  77.8 8.8 all-to-all-start
  87.4 1189.5 %all-to-all-done = bf16[512,8,6656]{0,2,1:T(8,128)(2,1)} async-done(((bf16[512,8,6656]{0,2,1:T(8,128)(2,1)}), bf16[512,8,6656]{0,2,1:T(8,128)(2,1)}, u32[]{:S(2)}, u32[]{:S(2)}) %all-to-all-start) | async-done | bytes 54525984 | tf_op jit(solution)/shard_map/all_to_all | solution.py:31
  1276.9 64.6 %copy.21 = bf16[8,512,6656]{2,1,0:T(8,128)(2,1)} copy(bf16[8,512,6656]{1,2,0:T(8,128)(2,1)} %bitcast.1) | data formatting | bytes 109051904 | tf_op jit(solution)/shard_map/all_to_all | solution.py:31
  1341.5 25.8 fusion.41
  1367.7 146.1 %all-reduce.8.cloned.1.call-done = f32[6656,256]{1,0:T(8,128)} async-done(((f32[6656,256]{1,0:T(8,128)}), f32[6656,256]{1,0:T(8,128)}) %all-reduce.8.cloned.1.call-update) | async-done | bytes 6815760 | tf_op jit(solution)/shard_map/psum | solution.py:40
  1513.8 16.6 fusion.42
  1531.0 55.0 %all-reduce.10.cloned.1.call-done = f32[256,256]{0,1:T(8,128)} async-done(((f32[256,256]{0,1:T(8,128)}), f32[256,256]{0,1:T(8,128)}) %all-reduce.10.cloned.1.call-update) | async-done | bytes 262160 | tf_op jit(solution)/shard_map/psum | solution.py:27
  1586.0 1.1 copy.23
  1587.1 1.0 fusion.11
  1588.1 11.7 cholesky.172
  1599.8 9.8 custom-call.15
  1610.2 11.7 cholesky.189
  1624.0 4.2 while.6
  1624.8 1.4 bitcast_dynamic-update-slice_fusion.6
  1626.8 1.4 bitcast_dynamic-update-slice_fusion.6
  1628.9 19.7 custom-call.16
  1648.5 5.2 fusion.7
  1653.7 6.5 convolution_subtract_fusion.2
  1660.3 4.5 fusion.20
  1664.7 24.3 convolution_bitcast_fusion.4
  1689.1 49.1 %reduce-scatter.4.cloned.1.call-done = f32[512,256]{0,1:T(8,128)} async-done(((f32[4096,256]{0,1:T(8,128)}), f32[512,256]{0,1:T(8,128)}) %reduce-scatter.4.cloned.1.call-update) | async-done | bytes 524304 | tf_op jit(solution)/shard_map/reduce_scatter | solution.py:43
  1738.2 1.8 convert_element_type.16
  1740.1 27.8 %all-gather.6.cloned.1.call-done = bf16[4096,256]{0,1:T(8,128)(2,1)} async-done(((bf16[512,256]{0,1:T(8,128)(2,1)}), bf16[4096,256]{0,1:T(8,128)(2,1)}) %all-gather.6.cloned.1.call-update) | async-done | bytes 2097168 | tf_op jit(solution)/shard_map/all_gather | solution.py:51
  1767.9 25.5 convolution_bitcast_fusion.1
  1793.5 146.3 %all-reduce.12.cloned.1.call-done = f32[6656,256]{0,1:T(8,128)} async-done(((f32[6656,256]{0,1:T(8,128)}), f32[6656,256]{0,1:T(8,128)}) %all-reduce.12.cloned.1.call-update) | async-done | bytes 6815760 | tf_op jit(solution)/shard_map/psum | solution.py:40
  1939.8 19.3 fusion.43
  1959.6 55.1 %all-reduce.14.cloned.1.call-done = f32[256,256]{0,1:T(8,128)} async-done(((f32[256,256]{0,1:T(8,128)}), f32[256,256]{0,1:T(8,128)}) %all-reduce.14.cloned.1.call-update) | async-done | bytes 262160 | tf_op jit(solution)/shard_map/psum | solution.py:27
  2014.7 1.1 copy.25
  2016.8 11.7 cholesky.206
  2028.6 9.8 custom-call.17
  2038.9 11.7 cholesky.223
  2053.2 4.2 while.7
  2054.0 1.4 bitcast_dynamic-update-slice_fusion.7
  2056.0 1.4 bitcast_dynamic-update-slice_fusion.7
  2058.1 19.7 custom-call.18
  2077.8 5.2 fusion.5
  2083.0 4.2 convolution_subtract_fusion.1
  2087.2 4.3 fusion.16
  2091.4 24.5 convolution_bitcast_fusion.3
  2116.0 49.1 %reduce-scatter.6.cloned.1.call-done = f32[512,256]{0,1:T(8,128)} async-done(((f32[4096,256]{0,1:T(8,128)}), f32[512,256]{0,1:T(8,128)}) %reduce-scatter.6.cloned.1.call-update) | async-done | bytes 524304 | tf_op jit(solution)/shard_map/reduce_scatter | solution.py:43
  2165.1 1.8 convert_element_type.18
  2167.0 28.0 %all-gather.8.cloned.1.call-done = bf16[4096,256]{0,1:T(8,128)(2,1)} async-done(((bf16[512,256]{0,1:T(8,128)(2,1)}), bf16[4096,256]{0,1:T(8,128)(2,1)}) %all-gather.8.cloned.1.call-update) | async-done | bytes 2097168 | tf_op jit(solution)/shard_map/all_gather | solution.py:51
  2194.9 25.5 convolution_bitcast_fusion
  2220.5 146.3 %all-reduce.16.cloned.1.call-done = f32[6656,256]{0,1:T(8,128)} async-done(((f32[6656,256]{0,1:T(8,128)}), f32[6656,256]{0,1:T(8,128)}) %all-reduce.16.cloned.1.call-update) | async-done | bytes 6815760 | tf_op jit(solution)/shard_map/psum | solution.py:40
  2366.8 19.3 fusion.44
  2386.6 55.1 %all-reduce.18.cloned.1.call-done = f32[256,256]{0,1:T(8,128)} async-done(((f32[256,256]{0,1:T(8,128)}), f32[256,256]{0,1:T(8,128)}) %all-reduce.18.cloned.1.call-update) | async-done | bytes 262160 | tf_op jit(solution)/shard_map/psum | solution.py:27
  2441.8 1.1 copy.28
  2442.9 1.0 fusion.9
  2443.9 11.7 cholesky.240
  2455.6 9.8 custom-call.19
  2465.9 11.7 cholesky.257
  2480.3 4.2 while.8
  2481.1 1.4 bitcast_dynamic-update-slice_fusion.8
  2483.1 1.4 bitcast_dynamic-update-slice_fusion.8
  2485.2 19.7 custom-call.20
  2504.9 5.2 fusion.3
  2510.0 4.2 convolution_subtract_fusion
  2514.2 4.9 fusion.12
  2519.2 25.4 convolution_bitcast_fusion.2
  2544.6 5.4 fusion
  2549.9 8.1 copy.31
  2558.0 35.7 %reduce-scatter.8.cloned.1.call-done = f32[512,256]{0,1:T(8,128)} async-done(((f32[4096,256]{0,1:T(8,128)}), f32[512,256]{0,1:T(8,128)}) %reduce-scatter.8.cloned.1.call-update) | async-done | bytes 524304 | tf_op jit(solution)/shard_map/reduce_scatter | solution.py:43
  2593.7 2.0 copy.30
  (81 shorter events, 14.8 us)
Async XLA Ops:
  77.8 1199.1 %all-to-all-start = ((bf16[512,8,6656]{0,2,1:T(8,128)(2,1)}), bf16[512,8,6656]{0,2,1:T(8,128)(2,1)}, u32[]{:S(2)}, u32[]{:S(2)}) async-start(bf16[512,8,6656]{0,2,1:T(8,128)(2,1)} %bitcast.124), calls=%async_computation | async-start | bytes 109051904 | tf_op jit(solution)/shard_map/all_to_all | solution.py:31
  86.6 1254.9 %all-gather.4.cloned.1.call-start = ((), (), s32[]{:S(2)}) async-start(), calls=%async_computation.4 | async-start | bytes 2359296 | tf_op jit(solution)/shard_map/all_gather | solution.py:38
  87.3 1426.5 %all-reduce.8.cloned.1.call-start = ((), (), s32[]{:S(2)}) async-start(), calls=%async_computation.5 | async-start | bytes 13631488 | tf_op jit(solution)/shard_map/psum | solution.py:40
  1367.4 218.6 %all-reduce.10.cloned.1.call-start = ((), (), s32[]{:S(2)}) async-start(), calls=%async_computation.6 | async-start | bytes 524288 | tf_op jit(solution)/shard_map/psum | solution.py:27
  1530.4 207.8 %reduce-scatter.4.cloned.1.call-start = ((), (), s32[]{:S(2)}) async-start(), calls=%async_computation.7 | async-start | bytes 4718592 | tf_op jit(solution)/shard_map/reduce_scatter | solution.py:43
  1628.2 0.7 copy-start.4
  1648.5 5.2 copy-start
  1689.1 78.8 %all-gather.6.cloned.1.call-start = ((), (), s32[]{:S(2)}) async-start(), calls=%async_computation.8 | async-start | bytes 2359296 | tf_op jit(solution)/shard_map/all_gather | solution.py:51
  1740.0 199.8 %all-reduce.12.cloned.1.call-start = ((), (), s32[]{:S(2)}) async-start(), calls=%async_computation.9 | async-start | bytes 13631488 | tf_op jit(solution)/shard_map/psum | solution.py:40
  1793.4 221.3 %all-reduce.14.cloned.1.call-start = ((), (), s32[]{:S(2)}) async-start(), calls=%async_computation.10 | async-start | bytes 524288 | tf_op jit(solution)/shard_map/psum | solution.py:27
  1959.1 206.0 %reduce-scatter.6.cloned.1.call-start = ((), (), s32[]{:S(2)}) async-start(), calls=%async_computation.11 | async-start | bytes 4718592 | tf_op jit(solution)/shard_map/reduce_scatter | solution.py:43
  2057.4 0.7 copy-start.5
  2077.8 5.2 copy-start.2
  2116.0 79.0 %all-gather.8.cloned.1.call-start = ((), (), s32[]{:S(2)}) async-start(), calls=%async_computation.12 | async-start | bytes 2359296 | tf_op jit(solution)/shard_map/all_gather | solution.py:51
  2166.9 199.9 %all-reduce.16.cloned.1.call-start = ((), (), s32[]{:S(2)}) async-start(), calls=%async_computation.13 | async-start | bytes 13631488 | tf_op jit(solution)/shard_map/psum | solution.py:40
  2220.5 221.3 %all-reduce.18.cloned.1.call-start = ((), (), s32[]{:S(2)}) async-start(), calls=%async_computation.14 | async-start | bytes 524288 | tf_op jit(solution)/shard_map/psum | solution.py:27
  2386.2 207.5 %reduce-scatter.8.cloned.1.call-start = ((), (), s32[]{:S(2)}) async-start(), calls=%async_computation.15 | async-start | bytes 4718592 | tf_op jit(solution)/shard_map/reduce_scatter | solution.py:43
  2484.5 0.7 copy-start.3
  2504.9 5.2 copy-start.1
Sparse Core Ops, SparseCore 0:
  89.0 49.5 all-gather.3
  1367.5 146.2 all-reduce.7
  1530.6 55.4 all-reduce.9
  1689.2 48.9 reduce-scatter.3
  1740.2 27.5 all-gather.5
  1793.5 146.1 all-reduce.11
  1959.2 55.4 all-reduce.13
  2116.1 48.9 reduce-scatter.5
  2167.3 27.6 all-gather.7
  2220.6 146.1 all-reduce.15
  2386.3 55.4 all-reduce.17
  2544.7 48.9 reduce-scatter.7
where the time goes:
time: 2610 us; the launch traced here: 2600 us
  waiting for transfers between devices  1980 us (76%)
  matrix products  252 us (10%)
  other arithmetic  174 us (7%)
  local copies, waits for them, and re-layouts  163 us (6%)
    all_to_all x1, waiting for transfers between devices, shards(): lax.all_to_all(gradient, 'col', split_axis=1, concat_axis=0, tiled=True)  1190 us
    psum x3, waiting for transfers between devices, shards(): summed = lax.psum(sketch, 'grad')  439 us
    psum x3, waiting for transfers between devices, gram_over_columns(): return lax.psum(partial_gram, 'col')  165 us
    reduce_scatter x3, waiting for transfers between devices, shards(): lax.psum_scatter(jnp.dot(blocks, basis_bf, preferred_element_type=jnp.flo...  134 us
    another operation x20, other arithmetic, orthonormal(): lower_factor = jnp.linalg.cholesky(gram)  103 us
    unnamed x15, local copies, waits for them, and re-layouts  82.9 us
    dot_general x3, matrix products, add_sketch(): lax.dot_general(blocks, row_piece, (((0,), (0,)), ((), ())), preferred_el...  76.9 us
    dot_general x3, matrix products, shards(): jnp.dot(blocks, basis_bf, preferred_element_type=jnp.float32)  74.2 us
  transfers between devices with their start and end apart: 13, of which 12 were waited for; matrix products, arithmetic and copies ran while one was open for 3% of the time, Pallas kernels for 0%

commit v1 on v0

--- a/solution.py
+++ b/solution.py
@@ -37,7 +37,9 @@
 
     sketch = add_sketch(lax.all_gather(test_matrix, "col", axis=0, tiled=True))
     for iteration in range(POWER + 1):
-        summed = lax.psum(sketch, "grad")
+        summed = sketch
+        for hop in (1, 2):
+            summed = summed + lax.ppermute(summed, "grad", [(dev, dev ^ hop) for dev in range(4)])
         basis_block = orthonormal(summed, gram_over_columns)
         basis_bf = basis_block.astype(jnp.bfloat16)
         reduced = lax.psum_scatter(

time: 2610 us -> 3060 us (1.17)
  waiting for transfers between devices: 1980 us -> 2420 us
    ppermute x0 -> x6, waiting for transfers between devices: none -> 881 us  [shards(): lax.ppermute(summed, 'grad', [(dev, dev ^ hop) for dev in range(4)])]
    psum x3 -> x0, waiting for transfers between devices: 439 us -> none  [shards(): summed = lax.psum(sketch, 'grad')]
    unnamed x15 -> x29, local copies, waits for them, and re-layouts: 82.9 us -> 91.2 us
  transfers between devices with their start and end apart: 13 -> 16, of which waited for: 12 -> 15; matrix products, arithmetic and copies ran while one was open for 3% -> 3% of each run, Pallas kernels for 0% -> 0%
where the time goes in v1:
time: 3060 us; the launch traced here: 3050 us
  waiting for transfers between devices  2420 us (79%)
  matrix products  224 us (7%)
  other arithmetic  198 us (6%)
  local copies, waits for them, and re-layouts  171 us (6%)
    all_to_all x1, waiting for transfers between devices, shards(): lax.all_to_all(gradient, 'col', split_axis=1, concat_axis=0, tiled=True)  1190 us
    ppermute x6, waiting for transfers between devices, shards(): lax.ppermute(summed, 'grad', [(dev, dev ^ hop) for dev in range(4)])  881 us
    psum x3, waiting for transfers between devices, gram_over_columns(): return lax.psum(partial_gram, 'col')  165 us
    reduce_scatter x3, waiting for transfers between devices, shards(): lax.psum_scatter(jnp.dot(blocks, basis_bf, preferred_element_type=jnp.flo...  132 us
    another operation x20, other arithmetic, orthonormal(): lower_factor = jnp.linalg.cholesky(gram)  103 us
    unnamed x29, local copies, waits for them, and re-layouts  91.2 us
    dot_general x3, matrix products, add_sketch(): lax.dot_general(blocks, row_piece, (((0,), (0,)), ((), ())), preferred_el...  78.4 us
    dot_general x3, matrix products, shards(): jnp.dot(blocks, basis_bf, preferred_element_type=jnp.float32)  77 us
  transfers between devices with their start and end apart: 16, of which 15 were waited for; matrix products, arithmetic and copies ran while one was open for 3% of the time, Pallas kernels for 0%

profile of v1, /device:TPU:0, one launch (start us, length us, event | category | flops | bytes accessed | tf_op | source)
XLA Modules:
  0.0 3054.8 jit_solution(4228706518478287738)
XLA Ops:
  7.2 70.5 %copy.20 = bf16[512,53248]{0,1:T(8,128)(2,1)} copy(bf16[512,53248]{1,0:T(8,128)(2,1)} %param.5) | data formatting | bytes 109051904 | tf_op args[0]
  77.6 8.8 all-to-all-start
  87.2 1189.5 %all-to-all-done = bf16[512,8,6656]{0,2,1:T(8,128)(2,1)} async-done(((bf16[512,8,6656]{0,2,1:T(8,128)(2,1)}), bf16[512,8,6656]{0,2,1:T(8,128)(2,1)}, u32[]{:S(2)}, u32[]{:S(2)}) %all-to-all-start) | async-done | bytes 54525984 | tf_op jit(solution)/shard_map/all_to_all | solution.py:31
  1276.7 64.7 %copy.21 = bf16[8,512,6656]{2,1,0:T(8,128)(2,1)} copy(bf16[8,512,6656]{1,2,0:T(8,128)(2,1)} %bitcast.1) | data formatting | bytes 109051904 | tf_op jit(solution)/shard_map/all_to_all | solution.py:31
  1341.4 26.2 fusion.44
  1367.6 2.2 collective-permute-start
  1369.8 146.7 %collective-permute-done = f32[6656,256]{1,0:T(8,128)S(1)} collective-permute-done((f32[6656,256]{1,0:T(8,128)}, f32[6656,256]{1,0:T(8,128)S(1)}, u32[]{:S(2)}, u32[]{:S(2)}) %collective-permute-start) | collective-permute-done | bytes 6815776 | tf_op jit(solution)/shard_map/ppermute | solution.py:42
  1516.5 3.8 add.47
  1522.2 146.0 %collective-permute-done.1 = f32[6656,256]{1,0:T(8,128)} collective-permute-done((f32[6656,256]{1,0:T(8,128)S(1)}, f32[6656,256]{1,0:T(8,128)}, u32[]{:S(2)}, u32[]{:S(2)}) %collective-permute-start.1) | collective-permute-done | bytes 6815776 | tf_op jit(solution)/shard_map/ppermute | solution.py:42
  1668.1 3.8 add.48
  1671.9 2.9 copy-done
  1674.8 12.2 fusion.45
  1687.1 55.4 %all-reduce.5.cloned.1.call-done = f32[256,256]{0,1:T(8,128)} async-done(((f32[256,256]{0,1:T(8,128)}), f32[256,256]{0,1:T(8,128)}) %all-reduce.5.cloned.1.call-update) | async-done | bytes 262160 | tf_op jit(solution)/shard_map/psum | solution.py:27
  1744.6 11.7 cholesky.172
  1756.4 9.8 custom-call.15
  1766.7 11.7 cholesky.189
  1780.5 4.0 while.6
  1784.5 19.7 custom-call.16
  1804.2 5.4 fusion.10
  1809.6 5.5 fusion.23
  1815.1 4.4 fusion.9
  1819.5 25.5 convolution_bitcast_fusion.4
  1845.0 49.1 %reduce-scatter.4.cloned.1.call-done = f32[512,256]{0,1:T(8,128)} async-done(((f32[4096,256]{0,1:T(8,128)}), f32[512,256]{0,1:T(8,128)}) %reduce-scatter.4.cloned.1.call-update) | async-done | bytes 524304 | tf_op jit(solution)/shard_map/reduce_scatter | solution.py:45
  1896.0 27.8 all-gather.6.cloned.1.call-done
  1923.8 26.1 convolution_bitcast_fusion.1
  1951.4 147.6 %collective-permute-done.2 = f32[6656,256]{0,1:T(8,128)S(1)} collective-permute-done((f32[6656,256]{0,1:T(8,128)}, f32[6656,256]{0,1:T(8,128)S(1)}, u32[]{:S(2)}, u32[]{:S(2)}) %collective-permute-start.2) | collective-permute-done | bytes 6815776 | tf_op jit(solution)/shard_map/ppermute | solution.py:42
  2099.0 4.0 add.49
  2104.6 146.7 %collective-permute-done.3 = f32[6656,256]{0,1:T(8,128)} collective-permute-done((f32[6656,256]{0,1:T(8,128)S(1)}, f32[6656,256]{0,1:T(8,128)}, u32[]{:S(2)}, u32[]{:S(2)}) %collective-permute-start.3) | collective-permute-done | bytes 6815776 | tf_op jit(solution)/shard_map/ppermute | solution.py:42
  2251.2 4.0 add.50
  2255.2 2.9 copy-done.2
  2258.1 6.3 fusion.46
  2264.6 54.8 %all-reduce.7.cloned.1.call-done = f32[256,256]{0,1:T(8,128)} async-done(((f32[256,256]{0,1:T(8,128)}), f32[256,256]{0,1:T(8,128)}) %all-reduce.7.cloned.1.call-update) | async-done | bytes 262160 | tf_op jit(solution)/shard_map/psum | solution.py:27
  2321.5 11.7 cholesky.206
  2333.2 9.8 custom-call.17
  2343.5 11.7 cholesky.223
  2357.8 4.1 while.7
  2361.9 19.7 custom-call.18
  2381.6 5.3 fusion.7
  2386.9 3.3 fusion.19
  2390.3 4.4 fusion.6
  2394.6 25.5 convolution_bitcast_fusion.3
  2420.2 49.1 %reduce-scatter.6.cloned.1.call-done = f32[512,256]{0,1:T(8,128)} async-done(((f32[4096,256]{0,1:T(8,128)}), f32[512,256]{0,1:T(8,128)}) %reduce-scatter.6.cloned.1.call-update) | async-done | bytes 524304 | tf_op jit(solution)/shard_map/reduce_scatter | solution.py:45
  2471.1 28.0 all-gather.8.cloned.1.call-done
  2499.1 26.1 convolution_bitcast_fusion
  2526.7 147.6 %collective-permute-done.4 = f32[6656,256]{0,1:T(8,128)S(1)} collective-permute-done((f32[6656,256]{0,1:T(8,128)}, f32[6656,256]{0,1:T(8,128)S(1)}, u32[]{:S(2)}, u32[]{:S(2)}) %collective-permute-start.4) | collective-permute-done | bytes 6815776 | tf_op jit(solution)/shard_map/ppermute | solution.py:42
  2674.3 4.0 add.51
  2679.9 146.7 %collective-permute-done.5 = f32[6656,256]{0,1:T(8,128)} collective-permute-done((f32[6656,256]{0,1:T(8,128)S(1)}, f32[6656,256]{0,1:T(8,128)}, u32[]{:S(2)}, u32[]{:S(2)}) %collective-permute-start.5) | collective-permute-done | bytes 6815776 | tf_op jit(solution)/shard_map/ppermute | solution.py:42
  2826.6 4.0 add.52
  2830.6 2.9 copy-done.1
  2833.4 6.3 fusion.47
  2840.0 54.8 %all-reduce.9.cloned.1.call-done = f32[256,256]{0,1:T(8,128)} async-done(((f32[256,256]{0,1:T(8,128)}), f32[256,256]{0,1:T(8,128)}) %all-reduce.9.cloned.1.call-update) | async-done | bytes 262160 | tf_op jit(solution)/shard_map/psum | solution.py:27
  2896.8 11.7 cholesky.240
  2908.6 9.8 custom-call.19
  2918.9 11.7 cholesky.257
  2933.2 4.1 while.8
  2937.3 19.7 custom-call.20
  2957.0 5.3 fusion.4
  2962.3 3.3 fusion.15
  2965.6 5.1 fusion.3
  2970.8 26.1 convolution_bitcast_fusion.2
  2998.8 5.4 fusion
  3004.2 8.1 copy.31
  3012.3 33.7 %reduce-scatter.8.cloned.1.call-done = f32[512,256]{0,1:T(8,128)} async-done(((f32[4096,256]{0,1:T(8,128)}), f32[512,256]{0,1:T(8,128)}) %reduce-scatter.8.cloned.1.call-update) | async-done | bytes 524304 | tf_op jit(solution)/shard_map/reduce_scatter | solution.py:45
  3046.0 2.0 copy.30
  (107 shorter events, 37.6 us)
Async XLA Ops:
  77.6 1199.1 %all-to-all-start = ((bf16[512,8,6656]{0,2,1:T(8,128)(2,1)}), bf16[512,8,6656]{0,2,1:T(8,128)(2,1)}, u32[]{:S(2)}, u32[]{:S(2)}) async-start(bf16[512,8,6656]{0,2,1:T(8,128)(2,1)} %bitcast.121), calls=%async_computation | async-start | bytes 109051904 | tf_op jit(solution)/shard_map/all_to_all | solution.py:31
  86.5 1255.0 %all-gather.4.cloned.1.call-start = ((), (), s32[]{:S(2)}) async-start(), calls=%async_computation.4 | async-start | bytes 2359296 | tf_op jit(solution)/shard_map/all_gather | solution.py:38
  87.2 1655.3 %all-reduce.5.cloned.1.call-start = ((), (), s32[]{:S(2)}) async-start(), calls=%async_computation.5 | async-start | bytes 524288 | tf_op jit(solution)/shard_map/psum | solution.py:27
  1367.6 148.9 %collective-permute-start = (f32[6656,256]{1,0:T(8,128)}, f32[6656,256]{1,0:T(8,128)S(1)}, u32[]{:S(2)}, u32[]{:S(2)}) collective-permute-start(f32[6656,256]{1,0:T(8,128)} %fusion.44), channel_id=1, source_target_pairs={{0,8},{8,0},{16,24},{24,16},{1,9},{9,1},{17,25},{25,17},{2,10},{10... | collective-permute-start | bytes 20447240 | tf_op jit(solution)/shard_map/ppermute | solution.py:42
  1520.3 147.8 %collective-permute-start.1 = (f32[6656,256]{1,0:T(8,128)S(1)}, f32[6656,256]{1,0:T(8,128)}, u32[]{:S(2)}, u32[]{:S(2)}) collective-permute-start(f32[6656,256]{1,0:T(8,128)S(1)} %add.47), channel_id=1, source_target_pairs={{0,16},{8,24},{16,0},{24,8},{1,17},{9,25},{17,1},{25,9},{2,18},{10... | collective-permute-start | bytes 20447240 | tf_op jit(solution)/shard_map/ppermute | solution.py:42
  1671.9 2.9 copy-start
  1687.1 207.0 %reduce-scatter.4.cloned.1.call-start = ((), (), s32[]{:S(2)}) async-start(), calls=%async_computation.6 | async-start | bytes 4718592 | tf_op jit(solution)/shard_map/reduce_scatter | solution.py:45
  1780.4 34.6 %slice-start = ((s8[6815744]{0:T(1024)(128)(4,1)}), s8[2621440]{0:T(1024)(128)(4,1)S(1)}, s32[]{:S(2)}) async-start(s8[6815744]{0:T(1024)(128)(4,1)} %bitcast.122), calls=%async_computation.13 | async-start | bytes 5242880
  1804.2 10.9 slice-start.1
  1809.6 9.9 copy-start.5
  1845.0 78.8 %all-gather.6.cloned.1.call-start = ((), (), s32[]{:S(2)}) async-start(), calls=%async_computation.7 | async-start | bytes 2359296 | tf_op jit(solution)/shard_map/all_gather | solution.py:53
  1895.9 423.5 %all-reduce.7.cloned.1.call-start = ((), (), s32[]{:S(2)}) async-start(), calls=%async_computation.8 | async-start | bytes 524288 | tf_op jit(solution)/shard_map/psum | solution.py:27
  1949.9 149.1 %collective-permute-start.2 = (f32[6656,256]{0,1:T(8,128)}, f32[6656,256]{0,1:T(8,128)S(1)}, u32[]{:S(2)}, u32[]{:S(2)}) collective-permute-start(f32[6656,256]{0,1:T(8,128)} %convolution_bitcast_fusion.1), channel_id=1, source_target_pairs={{0,8},{8,0},{16,24},{24,16},{1,9},{9,1},{17,25},{25,17},{2,10},{10... | collective-permute-start | bytes 20447240 | tf_op jit(solution)/shard_map/ppermute | solution.py:42
  2103.0 148.2 %collective-permute-start.3 = (f32[6656,256]{0,1:T(8,128)S(1)}, f32[6656,256]{0,1:T(8,128)}, u32[]{:S(2)}, u32[]{:S(2)}) collective-permute-start(f32[6656,256]{0,1:T(8,128)S(1)} %add.49), channel_id=1, source_target_pairs={{0,16},{8,24},{16,0},{24,8},{1,17},{9,25},{17,1},{25,9},{2,18},{10... | collective-permute-start | bytes 20447240 | tf_op jit(solution)/shard_map/ppermute | solution.py:42
  2255.2 2.9 copy-start.2
  2264.4 204.9 %reduce-scatter.6.cloned.1.call-start = ((), (), s32[]{:S(2)}) async-start(), calls=%async_computation.9 | async-start | bytes 4718592 | tf_op jit(solution)/shard_map/reduce_scatter | solution.py:45
  2357.8 32.4 %slice-start.4 = ((s8[6815744]{0:T(1024)(128)(4,1)}), s8[2621440]{0:T(1024)(128)(4,1)S(1)}, s32[]{:S(2)}) async-start(s8[6815744]{0:T(1024)(128)(4,1)} %bitcast.126), calls=%async_computation.17 | async-start | bytes 5242880
  2381.6 8.7 slice-start.5
  2386.9 7.7 copy-start.6
  2420.1 79.0 %all-gather.8.cloned.1.call-start = ((), (), s32[]{:S(2)}) async-start(), calls=%async_computation.10 | async-start | bytes 2359296 | tf_op jit(solution)/shard_map/all_gather | solution.py:53
  2471.1 423.7 %all-reduce.9.cloned.1.call-start = ((), (), s32[]{:S(2)}) async-start(), calls=%async_computation.11 | async-start | bytes 524288 | tf_op jit(solution)/shard_map/psum | solution.py:27
  2525.2 149.1 %collective-permute-start.4 = (f32[6656,256]{0,1:T(8,128)}, f32[6656,256]{0,1:T(8,128)S(1)}, u32[]{:S(2)}, u32[]{:S(2)}) collective-permute-start(f32[6656,256]{0,1:T(8,128)} %convolution_bitcast_fusion), channel_id=1, source_target_pairs={{0,8},{8,0},{16,24},{24,16},{1,9},{9,1},{17,25},{25,17},{2,10},{10... | collective-permute-start | bytes 20447240 | tf_op jit(solution)/shard_map/ppermute | solution.py:42
  2678.3 148.2 %collective-permute-start.5 = (f32[6656,256]{0,1:T(8,128)S(1)}, f32[6656,256]{0,1:T(8,128)}, u32[]{:S(2)}, u32[]{:S(2)}) collective-permute-start(f32[6656,256]{0,1:T(8,128)S(1)} %add.51), channel_id=1, source_target_pairs={{0,16},{8,24},{16,0},{24,8},{1,17},{9,25},{17,1},{25,9},{2,18},{10... | collective-permute-start | bytes 20447240 | tf_op jit(solution)/shard_map/ppermute | solution.py:42
  2830.5 2.9 copy-start.1
  2839.8 206.2 %reduce-scatter.8.cloned.1.call-start = ((), (), s32[]{:S(2)}) async-start(), calls=%async_computation.12 | async-start | bytes 4718592 | tf_op jit(solution)/shard_map/reduce_scatter | solution.py:45
  2933.2 32.4 %slice-start.2 = ((s8[6815744]{0:T(1024)(128)(4,1)}), s8[2621440]{0:T(1024)(128)(4,1)S(1)}, s32[]{:S(2)}) async-start(s8[6815744]{0:T(1024)(128)(4,1)} %bitcast.124), calls=%async_computation.15 | async-start | bytes 5242880
  2956.9 8.7 slice-start.3
  2962.3 8.5 copy-start.3
  2996.8 2.0 copy-start.4
Sparse Core Ops, SparseCore 0:
  88.9 49.5 all-gather.3
  1687.2 55.3 all-reduce.4
  1845.1 48.9 reduce-scatter.3
  1896.2 27.6 all-gather.5
  2264.5 54.8 all-reduce.6
  2420.3 48.9 reduce-scatter.5
  2471.5 27.5 all-gather.7
  2839.9 54.8 all-reduce.8
  2997.0 48.9 reduce-scatter.7
